TPU v7x, 1024 devices: a whole 4x4x32 slice. The times are simulated.
1024 devices in a mesh: mp: 8 (over x_hi, y), replica: 128 (over z, x_lo, core).
Axes of the slice: x: 4 (x_hi: 2, x_lo: 2; x = x_hi * 2 + x_lo), y: 4, z: 32, core: 2. Of those that a mesh axis runs over, the one named last changes fastest.
Arguments:
- pre: bfloat16 [128, 128, 12288], P('replica', None, 'mp'), may hold values from -6 to 6
- tok_keys: int32 [128, 128], P('replica'), may hold values from 0 to 16777215
- cotangent: bfloat16 [128, 128, 3072], P('replica', 'mp'), may hold values from -6 to 6
- w_out: bfloat16 [12288, 3072], P('mp'), may hold values from -0.0546875 to 0.0546875
- unit_keys: int32 [12288], P('mp'), may hold values from 0 to 16777215
- drop_salt: int32 [1], replicated, may hold values from 0 to 1073741823
- layer_key: int32 [1], replicated, may hold values from 0 to 63
- patch_count: int32 [128], P('replica'), may hold values from 64 to 128, as said below
Outputs:
- grad_pre: bfloat16 [128, 128, 12288], P('replica', None, 'mp')
- grad_bias: float32 [12288], P('mp')
Inputs may be any that keep to these rules, and one draw needn't show every extreme that they name: `patch_count`: at least one image uses all 128 patches.
All inputs are finite; a program needn't handle non-finite values.
Results may differ from a plain program's by a relative error of at most 0.007.
Values may be sent and summed in bfloat16 or wider, within the bound.
No kernel may reach another device: no remote copies, remote signals or barrier semaphores. Data moves between devices by JAX's collectives and lax.ppermute only.
A program may use at most 32 MiB of HBM per device.

v0:
```python
import jax
import jax.numpy as jnp
from jax import lax
from jax.sharding import PartitionSpec as P

keep_scale = 1.0 / 0.9


def scramble(value):
    value = value * jnp.int32(73244475)
    return value ^ lax.shift_right_logical(value, jnp.int32(16))


def mixing(value):
    return scramble(scramble(value))


def drop_scale(salt_value, layer_value, tok_row, unit_row):
    base = mixing(salt_value * jnp.int32(1103515245) + layer_value)
    row_code = mixing(base ^ tok_row)
    code = mixing(row_code[:, None] + unit_row[None, :] * jnp.int32(40503))
    return jnp.where(
        code & jnp.int32(65535) >= jnp.int32(6554), jnp.float32(keep_scale), jnp.float32(0.0)
    )


def gelu_tanh(value):
    return jax.nn.gelu(value, approximate=True)


def per_device(pre, tok_keys, cotangent, w_out, unit_keys, drop_salt, layer_key, patch_count):
    local_rows = cotangent.shape[1]
    patches = pre.shape[1]
    units = w_out.shape[0]
    replicas = lax.axis_size("replica")
    positions = lax.axis_index("mp") * local_rows + jnp.arange(local_rows, dtype=jnp.int32)
    valid = positions < patch_count[0]
    masked = jnp.where(valid[:, None], cotangent[0], jnp.zeros_like(cotangent[0]))
    scale = drop_scale(drop_salt[0], layer_key[0], tok_keys[0], unit_keys)
    pre_full = pre[0].astype(jnp.float32)
    part = lax.dot_general(
        lax.all_gather(masked, "mp", axis=0, tiled=True),
        w_out,
        (((1,), (1,)), ((), ())),
        preferred_element_type=jnp.float32,
    )
    _, gelu_back = jax.vjp(gelu_tanh, pre_full)
    grad_pre = gelu_back(part * scale)[0].astype(jnp.bfloat16)
    term = jnp.sum(grad_pre.astype(jnp.float32), axis=0)
    total = lax.psum(term, "replica")
    return (grad_pre.reshape(1, patches, units), total / jnp.float32(replicas))


def solution(mesh):
    return jax.shard_map(
        per_device,
        mesh=mesh,
        in_specs=(
            P("replica", None, "mp"),
            P("replica", None),
            P("replica", "mp", None),
            P("mp", None),
            P("mp"),
            P(),
            P(),
            P("replica"),
        ),
        out_specs=(P("replica", None, "mp"), P("mp")),
        check_vma=False,
    )
```

profile of v0, /device:TPU:1, one launch (start us, length us, event | category | flops | bytes accessed | tf_op | source)
XLA Modules:
  0.0 276.4 jit_solution(1049811382375092092)
XLA Ops:
  2.6 0.7 shift-right-logical_xor_fusion.2
  3.3 0.7 broadcast_multiply_fusion.1
  4.0 1.0 bitcast_select_fusion
  4.9 31.6 %all_gather.3 = bf16[128,3072]{1,0:T(8,128)(2,1)S(1)} all-gather(bf16[16,3072]{1,0:T(8,128)(2,1)S(1)} %bitcast_select_fusion), channel_id=1, replica_groups=mesh['mp'=8,'replica'=128] {'mp'}, dimensions={0}, use_global_device_ids=true | all-gather | bytes 884736 | tf_op jit(solution)/shard_map/all_gather | solution.py:42
  36.6 8.2 %convert_reduce_fusion = (f32[1536]{0:T(1024)S(1)}, bf16[128,1536]{1,0:T(8,128)(2,1)}) fusion(bf16[1,128,1536]{2,1,0:T(8,128)(2,1)} %param.8, s32[1536]{0:T(1024)S(1)} %broadcast_multiply_fusion.1, s32[128]{0:T(128)S(1)} %shift-right-logical_xor_fusion.2, bf16[128,3072]{1,0:T(8,128)(2,1)S(1)} %all_gather.3, bf16[1536,3072]{1,0:T(8,128)(2,1)} %param.11), kind=kOutput, calls=%fused_computation.19 | convolution fusion | flops 1214642688 | bytes 11022848 | tf_op jit(solution)/shard_map/dot_general | solution.py:41
  44.8 231.0 %psum.7 = f32[1536]{0:T(1024)S(1)} all-reduce(f32[1536]{0:T(1024)S(1)} %get-tuple-element.2), channel_id=1, replica_groups=mesh['mp'=8,'replica'=128] {'replica'}, use_global_device_ids=true, to_apply=%region_1.2 | all-reduce | flops 1536 | bytes 12288 | tf_op jit(solution)/shard_map/psum | solution.py:50
  275.8 0.6 broadcast_multiply_fusion
  (1 shorter events, 0.0 us)
where the time goes:
time: 277 us; the launch traced here: 276 us
  blocking collectives  263 us (95%)
  matrix products  8.23 us (3%)
  other arithmetic  2.94 us (1%)
    psum x1, blocking collectives, per_device(): total = lax.psum(term, 'replica')  231 us
    all_gather x1, blocking collectives, per_device(): lax.all_gather(masked, 'mp', axis=0, tiled=True)  31.6 us
    dot_general x1, matrix products, per_device(): lax.dot_general(lax.all_gather(masked, 'mp', axis=0, tiled=True), w_out,...  8.23 us

commit v1 on v0

v1 whole, which is shorter than its diff:
```python
import jax
import jax.numpy as jnp
from jax import lax
from jax.sharding import Mesh, PartitionSpec as P

keep_scale = 1.0 / 0.9


def scramble(value):
    value = value * jnp.int32(73244475)
    return value ^ lax.shift_right_logical(value, jnp.int32(16))


def mixing(value):
    return scramble(scramble(value))


def drop_scale(salt_value, layer_value, tok_row, unit_row):
    base = mixing(salt_value * jnp.int32(1103515245) + layer_value)
    row_code = mixing(base ^ tok_row)
    code = mixing(row_code[:, None] + unit_row[None, :] * jnp.int32(40503))
    return jnp.where(
        code & jnp.int32(65535) >= jnp.int32(6554), jnp.float32(keep_scale), jnp.float32(0.0)
    )


def gelu_tanh(value):
    return jax.nn.gelu(value, approximate=True)


MP = ("xh", "y")
REP = ("z", "xl", "c")


def per_device(pre, tok_keys, cotangent, w_out, unit_keys, drop_salt, layer_key, patch_count):
    local_rows = cotangent.shape[1]
    patches = pre.shape[1]
    units = w_out.shape[0]
    groups = patches // local_rows
    replicas = lax.axis_size(REP)
    positions = lax.axis_index(MP) * local_rows + jnp.arange(local_rows, dtype=jnp.int32)
    valid = positions < patch_count[0]
    masked = jnp.where(valid[:, None], cotangent[0], jnp.zeros_like(cotangent[0]))
    gathered = lax.all_to_all(
        jnp.broadcast_to(masked[None], (groups,) + masked.shape), MP, 0, 0, tiled=True
    ).reshape(patches, masked.shape[1])
    scale = drop_scale(drop_salt[0], layer_key[0], tok_keys[0], unit_keys)
    pre_full = pre[0].astype(jnp.float32)
    part = lax.dot_general(
        gathered,
        w_out,
        (((1,), (1,)), ((), ())),
        preferred_element_type=jnp.float32,
    )
    _, gelu_back = jax.vjp(gelu_tanh, pre_full)
    grad_pre = gelu_back(part * scale)[0].astype(jnp.bfloat16)
    term = jnp.sum(grad_pre.astype(jnp.float32), axis=0)
    total = lax.psum(term, ("xl", "c"))
    total = lax.psum(total, "z")
    return (grad_pre.reshape(1, patches, units), total / jnp.float32(replicas))


def solution(mesh):
    mp, replica = mesh.shape["mp"], mesh.shape["replica"]
    fine = Mesh(
        mesh.devices.reshape(2, mp // 2, replica // 4, 2, 2), MP + REP
    )
    return jax.shard_map(
        per_device,
        mesh=fine,
        in_specs=(
            P(REP, None, MP),
            P(REP, None),
            P(REP, MP, None),
            P(MP, None),
            P(MP),
            P(),
            P(),
            P(REP),
        ),
        out_specs=(P(REP, None, MP), P(MP)),
        check_vma=False,
    )
```

time: 277 us -> 108 us (0.39)
  the two profiles are of different devices: /device:TPU:1 before, /device:TPU:8 now
where the time goes in v1:
time: 108 us
  blocking collectives  70.3 us (65%)
  starting transfers between devices  16.5 us (15%)
  matrix products  8.23 us (8%)
  waiting for transfers between devices  6.28 us (6%)
  other arithmetic  2.95 us (3%)
  between operations  2.61 us (2%)
    psum x1, blocking collectives, per_device(): total = lax.psum(total, 'z')  64.5 us
    all_to_all x1, starting transfers between devices, per_device(): lax.all_to_all(jnp.broadcast_to(masked[None], (groups,) + masked.shape),...  16.5 us
    dot_general x1, matrix products, per_device(): lax.dot_general(gathered, w_out, (((1,), (1,)), ((), ())), preferred_elem...  8.23 us
    all_to_all x1, waiting for transfers between devices, per_device(): lax.all_to_all(jnp.broadcast_to(masked[None], (groups,) + masked.shape),...  6.28 us
    psum x1, blocking collectives, per_device(): total = lax.psum(term, ('xl', 'c'))  5.83 us
  transfers between devices with their start and end apart: 1, of which 1 were waited for; matrix products, arithmetic and copies ran while one was open for 1% of the time, Pallas kernels for 0%

profile of v1, /device:TPU:8, one launch (start us, length us, event | category | flops | bytes accessed | tf_op | source)
XLA Modules:
  0.0 107.9 jit_solution(7499418241954827175)
XLA Ops:
  1.3 1.0 select_bitcast_fusion
  2.3 1.0 broadcast_in_dim.33
  3.2 16.5 %all-to-all-start = ((bf16[8,16,3072]{2,1,0:T(8,128)(2,1)}), bf16[8,16,3072]{2,1,0:T(8,128)(2,1)S(1)}, u32[]{:S(2)}, u32[]{:S(2)}) async-start(bf16[8,16,3072]{2,1,0:T(8,128)(2,1)} %broadcast_in_dim.33), calls=%async_computation | async-start | bytes 1572864 | tf_op jit(solution)/shard_map/all_to_all | solution.py:44
  21.0 0.7 shift-right-logical_xor_fusion.2
  21.7 0.7 broadcast_multiply_fusion.1
  22.4 6.3 %all-to-all-done = bf16[8,16,3072]{2,1,0:T(8,128)(2,1)S(1)} async-done(((bf16[8,16,3072]{2,1,0:T(8,128)(2,1)}), bf16[8,16,3072]{2,1,0:T(8,128)(2,1)S(1)}, u32[]{:S(2)}, u32[]{:S(2)}) %all-to-all-start) | async-done | bytes 786464 | tf_op jit(solution)/shard_map/all_to_all | solution.py:44
  28.7 8.2 %convert_reduce_fusion = (f32[1536]{0:T(1024)S(1)}, bf16[128,1536]{1,0:T(8,128)(2,1)}) fusion(bf16[1,128,1536]{2,1,0:T(8,128)(2,1)} %param.8, s32[1536]{0:T(1024)S(1)} %broadcast_multiply_fusion.1, s32[128]{0:T(128)S(1)} %shift-right-logical_xor_fusion.2, bf16[128,3072]{1,0:T(8,128)(2,1)S(1)} %bitcast.14, bf16[1536,3072]{1,0:T(8,128)(2,1)} %param.11), kind=kOutput, calls=%fused_computation.19 | convolution fusion | flops 1214642688 | bytes 11022848 | tf_op jit(solution)/shard_map/dot_general | solution.py:49
  36.9 5.8 %psum.14 = f32[1536]{0:T(1024)S(1)} all-reduce(f32[1536]{0:T(1024)S(1)} %get-tuple-element.2), channel_id=1, replica_groups=mesh['xh'=2,'y'=4,'z'=32,'xl'=2,'c'=2] {'xl','c'}, use_global_device_ids=true, to_apply=%region_1.2 | all-reduce | flops 1536 | bytes 12288 | tf_op jit(solution)/shard_map/psum | solution.py:58
  42.8 64.5 %psum.15 = f32[1536]{0:T(1024)S(1)} all-reduce(f32[1536]{0:T(1024)S(1)} %psum.14), channel_id=1, replica_groups=mesh['xh'=2,'y'=4,'z'=32,'xl'=2,'c'=2] {'z'}, use_global_device_ids=true, to_apply=%region_2.3 | all-reduce | flops 1536 | bytes 12288 | tf_op jit(solution)/shard_map/psum | solution.py:59
  107.2 0.6 broadcast_multiply_fusion
  (1 shorter events, 0.0 us)
Async XLA Ops:
  3.2 25.5 %all-to-all-start = ((bf16[8,16,3072]{2,1,0:T(8,128)(2,1)}), bf16[8,16,3072]{2,1,0:T(8,128)(2,1)S(1)}, u32[]{:S(2)}, u32[]{:S(2)}) async-start(bf16[8,16,3072]{2,1,0:T(8,128)(2,1)} %broadcast_in_dim.33), calls=%async_computation | async-start | bytes 1572864 | tf_op jit(solution)/shard_map/all_to_all | solution.py:44

commit v2 on v1

--- a/solution.py
+++ b/solution.py
@@ -29,7 +29,7 @@
 
 
 MP = ("xh", "y")
-REP = ("z", "xl", "c")
+REP = ("zh", "zl", "xl", "c")
 
 
 def per_device(pre, tok_keys, cotangent, w_out, unit_keys, drop_salt, layer_key, patch_count):
@@ -56,14 +56,15 @@
     grad_pre = gelu_back(part * scale)[0].astype(jnp.bfloat16)
     term = jnp.sum(grad_pre.astype(jnp.float32), axis=0)
     total = lax.psum(term, ("xl", "c"))
-    total = lax.psum(total, "z")
+    total = lax.psum(total, "zl")
+    total = lax.psum(total, "zh")
     return (grad_pre.reshape(1, patches, units), total / jnp.float32(replicas))
 
 
 def solution(mesh):
     mp, replica = mesh.shape["mp"], mesh.shape["replica"]
     fine = Mesh(
-        mesh.devices.reshape(2, mp // 2, replica // 4, 2, 2), MP + REP
+        mesh.devices.reshape(2, mp // 2, replica // 16, 4, 2, 2), MP + REP
     )
     return jax.shard_map(
         per_device,

time: 108 us -> 87.2 us (0.81)
  blocking collectives: 70.3 us -> 49.3 us
    psum x1 -> x2, blocking collectives: 64.5 us -> 43.5 us  [the longest x1 35 us: per_device(): total = lax.psum(total, 'zh')]
  transfers between devices with their start and end apart: 1 -> 1, of which waited for: 1 -> 1; matrix products, arithmetic and copies ran while one was open for 1% -> 2% of each run, Pallas kernels for 0% -> 0%
where the time goes in v2:
time: 87.2 us; the launch traced here: 86.9 us
  blocking collectives  49.3 us (57%)
  starting transfers between devices  16.5 us (19%)
  matrix products  8.23 us (9%)
  waiting for transfers between devices  6.28 us (7%)
  other arithmetic  2.95 us (3%)
  between operations  2.62 us (3%)
  local copies, waits for them, and re-layouts  0.95 us (1%)
    psum x1, blocking collectives, per_device(): total = lax.psum(total, 'zh')  35 us
    all_to_all x1, starting transfers between devices, per_device(): lax.all_to_all(jnp.broadcast_to(masked[None], (groups,) + masked.shape),...  16.5 us
    psum x1, blocking collectives, per_device(): total = lax.psum(total, 'zl')  8.52 us
    dot_general x1, matrix products, per_device(): lax.dot_general(gathered, w_out, (((1,), (1,)), ((), ())), preferred_elem...  8.23 us
    all_to_all x1, waiting for transfers between devices, per_device(): lax.all_to_all(jnp.broadcast_to(masked[None], (groups,) + masked.shape),...  6.28 us
    psum x1, blocking collectives, per_device(): total = lax.psum(term, ('xl', 'c'))  5.83 us
  transfers between devices with their start and end apart: 1, of which 1 were waited for; matrix products, arithmetic and copies ran while one was open for 2% of the time, Pallas kernels for 0%

profile of v2, /device:TPU:8, one launch (start us, length us, event | category | flops | bytes accessed | tf_op | source)
XLA Modules:
  0.0 86.9 jit_solution(5921401703529684174)
XLA Ops:
  1.3 1.0 %select_bitcast_fusion = bf16[16,3072]{1,0:T(8,128)(2,1)S(1)} fusion(bf16[1,16,3072]{2,1,0:T(8,128)(2,1)} %param.10, pred[16]{0:T(512)(128)(4,1)S(1)} %add_compare_fusion), kind=kLoop, calls=%fused_computation.20 | loop fusion | flops 49152 | bytes 196624 | tf_op jit(solution)/shard_map/broadcast_in_dim | solution.py:45
  2.3 1.0 %broadcast_in_dim.33 = bf16[8,16,3072]{2,1,0:T(8,128)(2,1)} broadcast(bf16[16,3072]{1,0:T(8,128)(2,1)S(1)} %select_bitcast_fusion), dimensions={1,2} | broadcast | bytes 884736 | tf_op jit(solution)/shard_map/broadcast_in_dim | solution.py:45
  3.2 16.5 %all-to-all-start = ((bf16[8,16,3072]{2,1,0:T(8,128)(2,1)}), bf16[8,16,3072]{2,1,0:T(8,128)(2,1)S(1)}, u32[]{:S(2)}, u32[]{:S(2)}) async-start(bf16[8,16,3072]{2,1,0:T(8,128)(2,1)} %broadcast_in_dim.33), calls=%async_computation | async-start | bytes 1572864 | tf_op jit(solution)/shard_map/all_to_all | solution.py:44
  21.0 0.7 shift-right-logical_xor_fusion.2
  21.7 0.7 broadcast_multiply_fusion.1
  22.4 6.3 %all-to-all-done = bf16[8,16,3072]{2,1,0:T(8,128)(2,1)S(1)} async-done(((bf16[8,16,3072]{2,1,0:T(8,128)(2,1)}), bf16[8,16,3072]{2,1,0:T(8,128)(2,1)S(1)}, u32[]{:S(2)}, u32[]{:S(2)}) %all-to-all-start) | async-done | bytes 786464 | tf_op jit(solution)/shard_map/all_to_all | solution.py:44
  28.7 8.2 %convert_reduce_fusion = (f32[1536]{0:T(1024)S(1)}, bf16[128,1536]{1,0:T(8,128)(2,1)}) fusion(bf16[1,128,1536]{2,1,0:T(8,128)(2,1)} %param.8, s32[1536]{0:T(1024)S(1)} %broadcast_multiply_fusion.1, s32[128]{0:T(128)S(1)} %shift-right-logical_xor_fusion.2, bf16[128,3072]{1,0:T(8,128)(2,1)S(1)} %bitcast.14, bf16[1536,3072]{1,0:T(8,128)(2,1)} %param.11), kind=kOutput, calls=%fused_computation.19 | convolution fusion | flops 1214642688 | bytes 11022848 | tf_op jit(solution)/shard_map/dot_general | solution.py:49
  36.9 5.8 %psum.21 = f32[1536]{0:T(1024)S(1)} all-reduce(f32[1536]{0:T(1024)S(1)} %get-tuple-element.2), channel_id=1, replica_groups=mesh['xh'=2,'y'=4,'zh'=8,'zl'=4,'xl'=2,'c'=2] {'xl','c'}, use_global_device_ids=true, to_apply=%region_1.2 | all-reduce | flops 1536 | bytes 12288 | tf_op jit(solution)/shard_map/psum | solution.py:58
  42.8 8.5 %psum.22 = f32[1536]{0:T(1024)S(1)} all-reduce(f32[1536]{0:T(1024)S(1)} %psum.21), channel_id=1, replica_groups=mesh['xh'=2,'y'=4,'zh'=8,'zl'=4,'xl'=2,'c'=2] {'zl'}, use_global_device_ids=true, to_apply=%region_2.3 | all-reduce | flops 1536 | bytes 12288 | tf_op jit(solution)/shard_map/psum | solution.py:59
  51.3 35.0 %psum.23 = f32[1536]{0:T(1024)S(1)} all-reduce(f32[1536]{0:T(1024)S(1)} %psum.22), channel_id=1, replica_groups=mesh['xh'=2,'y'=4,'zh'=8,'zl'=4,'xl'=2,'c'=2] {'zh'}, use_global_device_ids=true, to_apply=%region_3.4 | all-reduce | flops 1536 | bytes 12288 | tf_op jit(solution)/shard_map/psum | solution.py:60
  86.3 0.6 broadcast_multiply_fusion
  (1 shorter events, 0.0 us)
Async XLA Ops:
  3.2 25.5 %all-to-all-start = ((bf16[8,16,3072]{2,1,0:T(8,128)(2,1)}), bf16[8,16,3072]{2,1,0:T(8,128)(2,1)S(1)}, u32[]{:S(2)}, u32[]{:S(2)}) async-start(bf16[8,16,3072]{2,1,0:T(8,128)(2,1)} %broadcast_in_dim.33), calls=%async_computation | async-start | bytes 1572864 | tf_op jit(solution)/shard_map/all_to_all | solution.py:44

commit v3 on v2

--- a/solution.py
+++ b/solution.py
@@ -29,7 +29,7 @@
 
 
 MP = ("xh", "y")
-REP = ("zh", "zl", "xl", "c")
+REP = ("zh", "zm", "zl", "xl", "c")
 
 
 def per_device(pre, tok_keys, cotangent, w_out, unit_keys, drop_salt, layer_key, patch_count):
@@ -57,6 +57,7 @@
     term = jnp.sum(grad_pre.astype(jnp.float32), axis=0)
     total = lax.psum(term, ("xl", "c"))
     total = lax.psum(total, "zl")
+    total = lax.psum(total, "zm")
     total = lax.psum(total, "zh")
     return (grad_pre.reshape(1, patches, units), total / jnp.float32(replicas))
 
@@ -64,7 +65,7 @@
 def solution(mesh):
     mp, replica = mesh.shape["mp"], mesh.shape["replica"]
     fine = Mesh(
-        mesh.devices.reshape(2, mp // 2, replica // 16, 4, 2, 2), MP + REP
+        mesh.devices.reshape(2, mp // 2, replica // 32, 2, 4, 2, 2), MP + REP
     )
     return jax.shard_map(
         per_device,

time: 87.2 us -> 93.5 us (1.072)
  blocking collectives: 49.3 us -> 55.6 us
    psum x0 -> x1, blocking collectives: none -> 8.91 us  [per_device(): total = lax.psum(total, 'zm')]
    psum x1, blocking collectives: 35 us -> 32.3 us  [per_device(): total = lax.psum(total, 'zh')]
  transfers between devices with their start and end apart: 1 -> 1, of which waited for: 1 -> 1; matrix products, arithmetic and copies ran while one was open for 2% -> 1% of each run, Pallas kernels for 0% -> 0%
where the time goes in v3:
time: 93.5 us; the launch traced here: 93.1 us
  blocking collectives  55.6 us (59%)
  starting transfers between devices  16.5 us (18%)
  matrix products  8.23 us (9%)
  waiting for transfers between devices  6.28 us (7%)
  other arithmetic  2.95 us (3%)
  between operations  2.62 us (3%)
  local copies, waits for them, and re-layouts  0.95 us (1%)
    psum x1, blocking collectives, per_device(): total = lax.psum(total, 'zh')  32.3 us
    all_to_all x1, starting transfers between devices, per_device(): lax.all_to_all(jnp.broadcast_to(masked[None], (groups,) + masked.shape),...  16.5 us
    psum x1, blocking collectives, per_device(): total = lax.psum(total, 'zm')  8.91 us
    psum x1, blocking collectives, per_device(): total = lax.psum(total, 'zl')  8.52 us
    dot_general x1, matrix products, per_device(): lax.dot_general(gathered, w_out, (((1,), (1,)), ((), ())), preferred_elem...  8.23 us
    all_to_all x1, waiting for transfers between devices, per_device(): lax.all_to_all(jnp.broadcast_to(masked[None], (groups,) + masked.shape),...  6.28 us
    psum x1, blocking collectives, per_device(): total = lax.psum(term, ('xl', 'c'))  5.83 us
  transfers between devices with their start and end apart: 1, of which 1 were waited for; matrix products, arithmetic and copies ran while one was open for 1% of the time, Pallas kernels for 0%

profile of v3, /device:TPU:8, one launch (start us, length us, event | category | flops | bytes accessed | tf_op | source)
XLA Modules:
  0.0 93.1 jit_solution(13299251304610537451)
XLA Ops:
  1.3 1.0 %select_bitcast_fusion = bf16[16,3072]{1,0:T(8,128)(2,1)S(1)} fusion(bf16[1,16,3072]{2,1,0:T(8,128)(2,1)} %param.10, pred[16]{0:T(512)(128)(4,1)S(1)} %add_compare_fusion), kind=kLoop, calls=%fused_computation.20 | loop fusion | flops 49152 | bytes 196624 | tf_op jit(solution)/shard_map/broadcast_in_dim | solution.py:45
  2.3 1.0 %broadcast_in_dim.33 = bf16[8,16,3072]{2,1,0:T(8,128)(2,1)} broadcast(bf16[16,3072]{1,0:T(8,128)(2,1)S(1)} %select_bitcast_fusion), dimensions={1,2} | broadcast | bytes 884736 | tf_op jit(solution)/shard_map/broadcast_in_dim | solution.py:45
  3.2 16.5 %all-to-all-start = ((bf16[8,16,3072]{2,1,0:T(8,128)(2,1)}), bf16[8,16,3072]{2,1,0:T(8,128)(2,1)S(1)}, u32[]{:S(2)}, u32[]{:S(2)}) async-start(bf16[8,16,3072]{2,1,0:T(8,128)(2,1)} %broadcast_in_dim.33), calls=%async_computation | async-start | bytes 1572864 | tf_op jit(solution)/shard_map/all_to_all | solution.py:44
  21.0 0.7 shift-right-logical_xor_fusion.2
  21.7 0.7 broadcast_multiply_fusion.1
  22.4 6.3 %all-to-all-done = bf16[8,16,3072]{2,1,0:T(8,128)(2,1)S(1)} async-done(((bf16[8,16,3072]{2,1,0:T(8,128)(2,1)}), bf16[8,16,3072]{2,1,0:T(8,128)(2,1)S(1)}, u32[]{:S(2)}, u32[]{:S(2)}) %all-to-all-start) | async-done | bytes 786464 | tf_op jit(solution)/shard_map/all_to_all | solution.py:44
  28.7 8.2 %convert_reduce_fusion = (f32[1536]{0:T(1024)S(1)}, bf16[128,1536]{1,0:T(8,128)(2,1)}) fusion(bf16[1,128,1536]{2,1,0:T(8,128)(2,1)} %param.8, s32[1536]{0:T(1024)S(1)} %broadcast_multiply_fusion.1, s32[128]{0:T(128)S(1)} %shift-right-logical_xor_fusion.2, bf16[128,3072]{1,0:T(8,128)(2,1)S(1)} %bitcast.14, bf16[1536,3072]{1,0:T(8,128)(2,1)} %param.11), kind=kOutput, calls=%fused_computation.19 | convolution fusion | flops 1214642688 | bytes 11022848 | tf_op jit(solution)/shard_map/dot_general | solution.py:49
  36.9 5.8 %psum.28 = f32[1536]{0:T(1024)S(1)} all-reduce(f32[1536]{0:T(1024)S(1)} %get-tuple-element.2), channel_id=1, replica_groups=mesh['xh'=2,'y'=4,'zh'=4,'zm'=2,'zl'=4,'xl'=2,'c'=2] {'xl','c'}, use_global_device_ids=true, to_apply=%region_1.2 | all-reduce | flops 1536 | bytes 12288 | tf_op jit(solution)/shard_map/psum | solution.py:58
  42.8 8.5 %psum.29 = f32[1536]{0:T(1024)S(1)} all-reduce(f32[1536]{0:T(1024)S(1)} %psum.28), channel_id=1, replica_groups=mesh['xh'=2,'y'=4,'zh'=4,'zm'=2,'zl'=4,'xl'=2,'c'=2] {'zl'}, use_global_device_ids=true, to_apply=%region_2.3 | all-reduce | flops 1536 | bytes 12288 | tf_op jit(solution)/shard_map/psum | solution.py:59
  51.3 8.9 %psum.30 = f32[1536]{0:T(1024)S(1)} all-reduce(f32[1536]{0:T(1024)S(1)} %psum.29), channel_id=1, replica_groups=mesh['xh'=2,'y'=4,'zh'=4,'zm'=2,'zl'=4,'xl'=2,'c'=2] {'zm'}, use_global_device_ids=true, to_apply=%region_3.4 | all-reduce | flops 1536 | bytes 12288 | tf_op jit(solution)/shard_map/psum | solution.py:60
  60.2 32.3 %psum.31 = f32[1536]{0:T(1024)S(1)} all-reduce(f32[1536]{0:T(1024)S(1)} %psum.30), channel_id=1, replica_groups=mesh['xh'=2,'y'=4,'zh'=4,'zm'=2,'zl'=4,'xl'=2,'c'=2] {'zh'}, use_global_device_ids=true, to_apply=%region_4.5 | all-reduce | flops 1536 | bytes 12288 | tf_op jit(solution)/shard_map/psum | solution.py:61
  92.5 0.6 broadcast_multiply_fusion
  (1 shorter events, 0.0 us)
Async XLA Ops:
  3.2 25.5 %all-to-all-start = ((bf16[8,16,3072]{2,1,0:T(8,128)(2,1)}), bf16[8,16,3072]{2,1,0:T(8,128)(2,1)S(1)}, u32[]{:S(2)}, u32[]{:S(2)}) async-start(bf16[8,16,3072]{2,1,0:T(8,128)(2,1)} %broadcast_in_dim.33), calls=%async_computation | async-start | bytes 1572864 | tf_op jit(solution)/shard_map/all_to_all | solution.py:44

commit v4 on v2

--- a/solution.py
+++ b/solution.py
@@ -53,7 +53,8 @@
         preferred_element_type=jnp.float32,
     )
     _, gelu_back = jax.vjp(gelu_tanh, pre_full)
-    grad_pre = gelu_back(part * scale)[0].astype(jnp.bfloat16)
+    factor = lax.optimization_barrier(gelu_back(scale)[0])
+    grad_pre = (part * factor).astype(jnp.bfloat16)
     term = jnp.sum(grad_pre.astype(jnp.float32), axis=0)
     total = lax.psum(term, ("xl", "c"))
     total = lax.psum(total, "zl")

time: 87.2 us -> 86.7 us (level)
  waiting for transfers between devices: 6.28 us -> 4.47 us
  other arithmetic: 2.95 us -> 4.76 us
    all_to_all x1, waiting for transfers between devices: 6.28 us -> 4.47 us  [per_device(): lax.all_to_all(jnp.broadcast_to(masked[None], (groups,) + masked.shape),...]
    add_any x0 -> x1, other arithmetic: none -> 1.81 us  [gelu_tanh(): return jax.nn.gelu(value, approximate=True)]
  transfers between devices with their start and end apart: 1 -> 1, of which waited for: 1 -> 1; matrix products, arithmetic and copies ran while one was open for 2% -> 4% of each run, Pallas kernels for 0% -> 0%
where the time goes in v4:
time: 86.7 us; the launch traced here: 86.3 us
  blocking collectives  49.3 us (57%)
  starting transfers between devices  16.5 us (19%)
  matrix products  7.64 us (9%)
  other arithmetic  4.76 us (5%)
  waiting for transfers between devices  4.47 us (5%)
  between operations  2.62 us (3%)
  local copies, waits for them, and re-layouts  0.95 us (1%)
    psum x1, blocking collectives, per_device(): total = lax.psum(total, 'zh')  35 us
    all_to_all x1, starting transfers between devices, per_device(): lax.all_to_all(jnp.broadcast_to(masked[None], (groups,) + masked.shape),...  16.5 us
    psum x1, blocking collectives, per_device(): total = lax.psum(total, 'zl')  8.52 us
    dot_general x1, matrix products, per_device(): lax.dot_general(gathered, w_out, (((1,), (1,)), ((), ())), preferred_elem...  7.64 us
    psum x1, blocking collectives, per_device(): total = lax.psum(term, ('xl', 'c'))  5.83 us
    all_to_all x1, waiting for transfers between devices, per_device(): lax.all_to_all(jnp.broadcast_to(masked[None], (groups,) + masked.shape),...  4.47 us
    add_any x1, other arithmetic, gelu_tanh(): return jax.nn.gelu(value, approximate=True)  1.81 us
  transfers between devices with their start and end apart: 1, of which 1 were waited for; matrix products, arithmetic and copies ran while one was open for 4% of the time, Pallas kernels for 0%

profile of v4, /device:TPU:8, one launch (start us, length us, event | category | flops | bytes accessed | tf_op | source)
XLA Modules:
  0.0 86.3 jit_solution(18001822782001859412)
XLA Ops:
  1.3 1.0 %select_bitcast_fusion = bf16[16,3072]{1,0:T(8,128)(2,1)S(1)} fusion(bf16[1,16,3072]{2,1,0:T(8,128)(2,1)} %param.10, pred[16]{0:T(512)(128)(4,1)S(1)} %add_compare_fusion), kind=kLoop, calls=%fused_computation.22 | loop fusion | flops 49152 | bytes 196624 | tf_op jit(solution)/shard_map/broadcast_in_dim | solution.py:45
  2.3 1.0 %broadcast_in_dim.33 = bf16[8,16,3072]{2,1,0:T(8,128)(2,1)} broadcast(bf16[16,3072]{1,0:T(8,128)(2,1)S(1)} %select_bitcast_fusion), dimensions={1,2} | broadcast | bytes 884736 | tf_op jit(solution)/shard_map/broadcast_in_dim | solution.py:45
  3.2 16.5 %all-to-all-start = ((bf16[8,16,3072]{2,1,0:T(8,128)(2,1)}), bf16[8,16,3072]{2,1,0:T(8,128)(2,1)S(1)}, u32[]{:S(2)}, u32[]{:S(2)}) async-start(bf16[8,16,3072]{2,1,0:T(8,128)(2,1)} %broadcast_in_dim.33), calls=%async_computation | async-start | bytes 1572864 | tf_op jit(solution)/shard_map/all_to_all | solution.py:44
  21.0 0.7 broadcast_multiply_fusion.1
  21.8 0.7 shift-right-logical_xor_fusion.2
  22.4 1.8 %fusion.3 = f32[128,1536]{1,0:T(8,128)S(1)} fusion(bf16[1,128,1536]{2,1,0:T(8,128)(2,1)} %param.8, s32[1536]{0:T(1024)S(1)} %broadcast_multiply_fusion.1, s32[128]{0:T(128)S(1)} %shift-right-logical_xor_fusion.2), kind=kLoop, calls=%fused_computation.11 | loop fusion | flops 5898240 | bytes 1186304 | tf_op jit(solution)/shard_map/transpose(jvp())/add_any | solution.py:28
  24.2 4.5 %all-to-all-done = bf16[8,16,3072]{2,1,0:T(8,128)(2,1)S(1)} async-done(((bf16[8,16,3072]{2,1,0:T(8,128)(2,1)}), bf16[8,16,3072]{2,1,0:T(8,128)(2,1)S(1)}, u32[]{:S(2)}, u32[]{:S(2)}) %all-to-all-start) | async-done | bytes 786464 | tf_op jit(solution)/shard_map/all_to_all | solution.py:44
  28.7 7.6 %convert_reduce_fusion = (f32[1536]{0:T(1024)S(1)}, bf16[128,1536]{1,0:T(8,128)(2,1)}) fusion(f32[128,1536]{1,0:T(8,128)S(1)} %fusion.3, bf16[128,3072]{1,0:T(8,128)(2,1)S(1)} %bitcast.14, bf16[1536,3072]{1,0:T(8,128)(2,1)} %param.11), kind=kOutput, calls=%fused_computation.21 | convolution fusion | flops 1208744448 | bytes 11409408 | tf_op jit(solution)/shard_map/dot_general | solution.py:49
  36.3 5.8 %psum.21 = f32[1536]{0:T(1024)S(1)} all-reduce(f32[1536]{0:T(1024)S(1)} %get-tuple-element.2), channel_id=1, replica_groups=mesh['xh'=2,'y'=4,'zh'=8,'zl'=4,'xl'=2,'c'=2] {'xl','c'}, use_global_device_ids=true, to_apply=%region_1.2 | all-reduce | flops 1536 | bytes 12288 | tf_op jit(solution)/shard_map/psum | solution.py:59
  42.2 8.5 %psum.22 = f32[1536]{0:T(1024)S(1)} all-reduce(f32[1536]{0:T(1024)S(1)} %psum.21), channel_id=1, replica_groups=mesh['xh'=2,'y'=4,'zh'=8,'zl'=4,'xl'=2,'c'=2] {'zl'}, use_global_device_ids=true, to_apply=%region_2.3 | all-reduce | flops 1536 | bytes 12288 | tf_op jit(solution)/shard_map/psum | solution.py:60
  50.7 35.0 %psum.23 = f32[1536]{0:T(1024)S(1)} all-reduce(f32[1536]{0:T(1024)S(1)} %psum.22), channel_id=1, replica_groups=mesh['xh'=2,'y'=4,'zh'=8,'zl'=4,'xl'=2,'c'=2] {'zh'}, use_global_device_ids=true, to_apply=%region_3.4 | all-reduce | flops 1536 | bytes 12288 | tf_op jit(solution)/shard_map/psum | solution.py:61
  85.7 0.6 broadcast_multiply_fusion
  (1 shorter events, 0.0 us)
Async XLA Ops:
  3.2 25.5 %all-to-all-start = ((bf16[8,16,3072]{2,1,0:T(8,128)(2,1)}), bf16[8,16,3072]{2,1,0:T(8,128)(2,1)S(1)}, u32[]{:S(2)}, u32[]{:S(2)}) async-start(bf16[8,16,3072]{2,1,0:T(8,128)(2,1)} %broadcast_in_dim.33), calls=%async_computation | async-start | bytes 1572864 | tf_op jit(solution)/shard_map/all_to_all | solution.py:44
